TPU v7x, 256 devices: a whole 4x4x8 slice. The times are simulated.
256 devices in a mesh: rep: 16 (over x_hi, z), fsdp: 16 (over x_lo, y, core).
Axes of the slice: x: 4 (x_hi: 2, x_lo: 2; x = x_hi * 2 + x_lo), y: 4, z: 8, core: 2. Of those that a mesh axis runs over, the one named last changes fastest.
Arguments:
- outer_start: float32 [2048, 8192], P(None, 'fsdp'), may hold values from -6 to 6
- local_weights: bfloat16 [16, 2048, 8192], P('rep', None, 'fsdp'), may hold values from -9 to 9
- momentum: float32 [2048, 8192], P('rep', 'fsdp'), may hold values from -0.6 to 0.6
Outputs:
- new_weights: bfloat16 [2048, 8192], P(None, 'fsdp')
- new_master: float32 [2048, 8192], P('rep', 'fsdp')
- new_momentum: float32 [2048, 8192], P('rep', 'fsdp')
All inputs are finite; a program needn't handle non-finite values.
Results may differ from a plain program's by a relative error of at most 0.0045.
Values may be sent and summed in bfloat16 or wider, within the bound.
No kernel may reach another device: no remote copies, remote signals or barrier semaphores. Data moves between devices by JAX's collectives and lax.ppermute only.
A program may use at most 64 MiB of HBM per device.

v0:
```python
import jax
import jax.numpy as jnp
from jax import lax
from jax.sharding import PartitionSpec as P

D = 8192
clip_level = 0.03
outer_rate = 0.7
momentum_coef = 0.9
eps_value = 1e-06


def make_difference(outer_rows, local_rows):
    rounded = (outer_rows - local_rows.astype(jnp.float32)).astype(jnp.bfloat16)
    rounded = lax.optimization_barrier(rounded)
    return rounded.astype(jnp.float32)


def outer_update(own_outer, outer_grad, unit_squares, momentum_rows):
    factor = jnp.minimum(1.0, clip_level / jnp.sqrt(unit_squares / D + eps_value))
    clipped = outer_grad * factor[:, None]
    new_momentum = momentum_coef * momentum_rows + clipped
    new_master = own_outer - outer_rate * (clipped + momentum_coef * new_momentum)
    return (new_master, new_momentum)


def on_device(outer_start, local_weights, momentum):
    local_shard = local_weights[0]
    replicas = lax.axis_size("rep")
    owner = lax.axis_index("rep")
    own_rows = outer_start.shape[0] // replicas
    summed = lax.psum_scatter(
        make_difference(outer_start, local_shard).astype(jnp.bfloat16),
        "rep",
        scatter_dimension=0,
        tiled=True,
    ).astype(jnp.float32)
    own_outer = lax.dynamic_slice_in_dim(outer_start, owner * own_rows, own_rows, 0)
    outer_grad = summed / replicas
    unit_squares = lax.psum(jnp.sum(outer_grad * outer_grad, axis=1), "fsdp")
    new_master, new_momentum = outer_update(own_outer, outer_grad, unit_squares, momentum)
    new_weights = lax.all_gather(new_master.astype(jnp.bfloat16), "rep", axis=0, tiled=True)
    return (new_weights, new_master, new_momentum)


def solution(mesh):
    return jax.shard_map(
        on_device,
        mesh=mesh,
        in_specs=(P(None, "fsdp"), P("rep", None, "fsdp"), P("rep", "fsdp")),
        out_specs=(P(None, "fsdp"), P("rep", "fsdp"), P("rep", "fsdp")),
        check_vma=False,
    )
```

profile of v0, /device:TPU:8, one launch (start us, length us, event | category | flops | bytes accessed | tf_op | source)
XLA Modules:
  0.0 344.7 jit_solution(3331967806520791519)
XLA Ops:
  7.2 0.0 reduce-scatter.2.cloned.1.call-start
  7.2 4.9 %fusion = bf16[2048,512]{1,0:T(8,128)(2,1)} fusion(f32[2048,512]{1,0:T(8,128)} %param.3, bf16[1,2048,512]{2,1,0:T(8,128)(2,1)} %param.4), kind=kLoop, calls=%fused_computation.1 | loop fusion | flops 3145728 | bytes 8388608 | tf_op jit(solution)/shard_map/convert_element_type | solution.py:14
  12.1 0.0 copy-start
  12.1 0.0 reduce-scatter.2.cloned.1.call-update
  12.1 0.0 all-gather.2.cloned.1.call-start
  12.2 211.4 %reduce-scatter.2.cloned.1.call-done = bf16[128,512]{1,0:T(8,128)(2,1)} async-done(((bf16[2048,512]{1,0:T(8,128)(2,1)}), bf16[128,512]{1,0:T(8,128)(2,1)}) %reduce-scatter.2.cloned.1.call-update) | async-done | bytes 131088 | tf_op jit(solution)/shard_map/reduce_scatter | solution.py:32
  223.6 1.0 fusion.6
  224.6 23.3 %psum.7 = f32[128]{0:T(128)S(1)} all-reduce(f32[128]{0:T(128)S(1)} %fusion.6), channel_id=1, replica_groups=mesh['rep'=16,'fsdp'=16] {'fsdp'}, use_global_device_ids=true, to_apply=%region_2.0 | all-reduce | flops 128 | bytes 1024 | tf_op jit(solution)/shard_map/psum | solution.py:40
  247.9 0.0 copy-done
  247.9 2.0 fusion.7
  249.9 0.0 all-gather.2.cloned.1.call-update
  249.9 84.9 %all-gather.2.cloned.1.call-done = bf16[2048,512]{1,0:T(8,128)(2,1)} async-done(((bf16[128,512]{1,0:T(8,128)(2,1)}), bf16[2048,512]{1,0:T(8,128)(2,1)}) %all-gather.2.cloned.1.call-update) | async-done | bytes 2097168 | tf_op jit(solution)/shard_map/all_gather | solution.py:42
  334.8 3.0 copy.7
  (1 shorter events, 0.0 us)
Async XLA Ops:
  7.2 216.4 %reduce-scatter.2.cloned.1.call-start = ((), (), s32[]{:S(2)}) async-start(), calls=%async_computation.1 | async-start | bytes 2228224 | tf_op jit(solution)/shard_map/reduce_scatter | solution.py:32
  12.1 235.8 %copy-start = (f32[128,512]{1,0:T(8,128)S(1)}, f32[128,512]{1,0:T(8,128)}, u32[]{:S(2)}) copy-start(f32[128,512]{1,0:T(8,128)} %param.5) | copy-start | bytes 786436
  12.1 322.7 %all-gather.2.cloned.1.call-start = ((), (), s32[]{:S(2)}) async-start(), calls=%async_computation.2 | async-start | bytes 2228224 | tf_op jit(solution)/shard_map/all_gather | solution.py:42
Sparse Core Ops, SparseCore 0:
  12.5 211.0 reduce-scatter.1
  250.0 84.7 all-gather.1
where the time goes:
time: 345 us
  waiting for transfers between devices  296 us (86%)
  blocking collectives  23.3 us (7%)
  between operations  14 us (4%)
  other arithmetic  7.92 us (2%)
    reduce_scatter x1, waiting for transfers between devices, on_device(): lax.psum_scatter(make_difference(outer_start, local_shard).astype(jnp.bfl...  211 us
    all_gather x1, waiting for transfers between devices, on_device(): lax.all_gather(new_master.astype(jnp.bfloat16), 'rep', axis=0, tiled=True)  84.9 us
    psum x1, blocking collectives, on_device(): unit_squares = lax.psum(jnp.sum(outer_grad * outer_grad, axis=1), 'fsdp')  23.3 us
  transfers between devices with their start and end apart: 2, of which 2 were waited for; matrix products, arithmetic and copies ran while one was open for 0% of the time, Pallas kernels for 0%

commit v1 on v0

--- a/solution.py
+++ b/solution.py
@@ -39,7 +39,9 @@
     outer_grad = summed / replicas
     unit_squares = lax.psum(jnp.sum(outer_grad * outer_grad, axis=1), "fsdp")
     new_master, new_momentum = outer_update(own_outer, outer_grad, unit_squares, momentum)
-    new_weights = lax.all_gather(new_master.astype(jnp.bfloat16), "rep", axis=0, tiled=True)
+    own = new_master.astype(jnp.bfloat16)
+    stack = jnp.stack([own] * lax.axis_size("rep"))
+    new_weights = jnp.concatenate(lax.all_to_all(stack, "rep", 0, 0), axis=0)
     return (new_weights, new_master, new_momentum)
 
 

time: 345 us -> 318 us (0.922)
  waiting for transfers between devices: 296 us -> 211 us
  blocking collectives: 23.3 us -> 79.7 us
    all_gather x1 -> x0, waiting for transfers between devices: 84.9 us -> none  [on_device(): lax.all_gather(new_master.astype(jnp.bfloat16), 'rep', axis=0, tiled=True)]
    all_to_all x0 -> x1, blocking collectives: none -> 56.4 us  [on_device(): new_weights = jnp.concatenate(lax.all_to_all(stack, 'rep', 0, 0), axis=0)]
  transfers between devices with their start and end apart: 2 -> 1, of which waited for: 2 -> 1; matrix products, arithmetic and copies ran while one was open for 0% -> 0% of each run, Pallas kernels for 0% -> 0%
where the time goes in v1:
time: 318 us; the launch traced here: 315 us
  waiting for transfers between devices  211 us (66%)
  blocking collectives  79.7 us (25%)
  between operations  14 us (4%)
  other arithmetic  7.88 us (2%)
    reduce_scatter x1, waiting for transfers between devices, on_device(): lax.psum_scatter(make_difference(outer_start, local_shard).astype(jnp.bfl...  211 us
    all_to_all x1, blocking collectives, on_device(): new_weights = jnp.concatenate(lax.all_to_all(stack, 'rep', 0, 0), axis=0)  56.4 us
    psum x1, blocking collectives, on_device(): unit_squares = lax.psum(jnp.sum(outer_grad * outer_grad, axis=1), 'fsdp')  23.3 us
  transfers between devices with their start and end apart: 1, of which 1 were waited for; matrix products, arithmetic and copies ran while one was open for 0% of the time, Pallas kernels for 0%

profile of v1, /device:TPU:8, one launch (start us, length us, event | category | flops | bytes accessed | tf_op | source)
XLA Modules:
  0.0 314.6 jit_solution(8097090104500927170)
XLA Ops:
  7.2 0.0 reduce-scatter.2.cloned.1.call-start
  7.2 4.9 %fusion = bf16[2048,512]{1,0:T(8,128)(2,1)} fusion(f32[2048,512]{1,0:T(8,128)} %param.3, bf16[1,2048,512]{2,1,0:T(8,128)(2,1)} %param.4), kind=kLoop, calls=%fused_computation.1 | loop fusion | flops 3145728 | bytes 8388608 | tf_op jit(solution)/shard_map/convert_element_type | solution.py:14
  12.1 0.0 copy-start
  12.1 0.0 reduce-scatter.2.cloned.1.call-update
  12.1 211.4 %reduce-scatter.2.cloned.1.call-done = bf16[128,512]{1,0:T(8,128)(2,1)} async-done(((bf16[2048,512]{1,0:T(8,128)(2,1)}), bf16[128,512]{1,0:T(8,128)(2,1)}) %reduce-scatter.2.cloned.1.call-update) | async-done | bytes 131088 | tf_op jit(solution)/shard_map/reduce_scatter | solution.py:32
  223.6 1.0 fusion.6
  224.6 23.3 %psum.7 = f32[128]{0:T(128)S(1)} all-reduce(f32[128]{0:T(128)S(1)} %fusion.6), channel_id=1, replica_groups=mesh['rep'=16,'fsdp'=16] {'fsdp'}, use_global_device_ids=true, to_apply=%region_2.0 | all-reduce | flops 128 | bytes 1024 | tf_op jit(solution)/shard_map/psum | solution.py:40
  247.9 0.0 copy-done
  247.9 1.9 fusion.7
  249.8 0.2 stack.2
  250.0 56.4 %all_to_all.5 = bf16[16,128,512]{2,1,0:T(8,128)(2,1)S(1)} all-to-all(bf16[16,128,512]{2,1,0:T(8,128)(2,1)S(1)} %stack.2), channel_id=1, replica_groups=mesh['rep'=16,'fsdp'=16] {'rep'}, dimensions={0} | all-to-all | bytes 4194304 | tf_op jit(solution)/shard_map/all_to_all | solution.py:44
  306.5 1.3 copy.7
  (1 shorter events, 0.0 us)
Async XLA Ops:
  7.2 216.4 %reduce-scatter.2.cloned.1.call-start = ((), (), s32[]{:S(2)}) async-start(), calls=%async_computation.2 | async-start | bytes 2228224 | tf_op jit(solution)/shard_map/reduce_scatter | solution.py:32
  12.1 235.8 %copy-start = (f32[128,512]{1,0:T(8,128)S(1)}, f32[128,512]{1,0:T(8,128)}, u32[]{:S(2)}) copy-start(f32[128,512]{1,0:T(8,128)} %param.5) | copy-start | bytes 786436
Sparse Core Ops, SparseCore 0:
  12.5 211.0 reduce-scatter.1
